TPU v7x, 128 devices: a whole 4x4x4 slice. The times are simulated.
128 devices in a mesh: sta: 2 (over x_lo), gx: 16 (over x_hi, z, core), gy: 4 (over y).
Axes of the slice: x: 4 (x_hi: 2, x_lo: 2; x = x_hi * 2 + x_lo), y: 4, z: 4, core: 2. Of those that a mesh axis runs over, the one named last changes fastest.
Arguments:
- record: float32 [128, 1024], replicated, may hold values from -6 to 6
- shifts: int32 [128, 256], P(None, 'gx'), may hold values from 0 to 1022
- station_group: int32 [128], replicated, may hold values from 0 to 7
- weights: bfloat16 [128, 256, 512], P('sta', 'gy'), may hold values from -6 to 6
- psf_real: float32 [256, 256, 512], P(None, 'gx', 'gy'), may hold values from -6 to 6
- psf_imag: float32 [256, 256, 512], P(None, 'gx', 'gy'), may hold values from -6 to 6
Outputs:
- image: float32 [2, 256, 256, 512], P('sta', 'gx', 'gy')
All inputs are finite; a program needn't handle non-finite values.
Results may differ from a plain program's by a relative error of at most 0.0029.
Values may be sent and summed in bfloat16 or wider, within the bound.
No kernel may reach another device: no remote copies, remote signals or barrier semaphores. Data moves between devices by JAX's collectives and lax.ppermute only.
A program may use at most 128 MiB of HBM per device.

v0:
```python
import math
import jax
import jax.numpy as jnp
from jax import lax
from jax.sharding import PartitionSpec as P

T_DEV = 1
NZ = 256
NX = 256
GROUPS = 8
NOISE_POWER = 0.25
HIGHEST = lax.Precision.HIGHEST


def station_counts(station_group):
    labels = jnp.arange(GROUPS, dtype=jnp.int32)
    onehot = (station_group[:, None] == labels[None, :]).astype(jnp.float32)
    totals = jnp.sum(onehot, axis=0)
    return jnp.dot(onehot, totals, precision=HIGHEST)


def coefficients(record, shifts, per_station, first_time, num_times):
    times_range = first_time + jnp.arange(num_times, dtype=jnp.int32)
    positions = shifts[:, :, None] + times_range[None, None, :]
    values = jnp.take_along_axis(record, positions.reshape(positions.shape[0], -1), axis=1)
    scaled = values.reshape(positions.shape) / per_station[:, None, None]
    return jnp.transpose(scaled, (2, 1, 0)).astype(jnp.bfloat16)


def fourier_parts(length, scale):
    indices = jnp.arange(length, dtype=jnp.int32)
    product = indices[:, None] * indices[None, :] % length
    angles = product.astype(jnp.float32) * (2.0 * math.pi / length)
    return (jnp.cos(angles) * scale, jnp.sin(angles) * scale)


def complex_table(length, forward):
    if forward:
        cosine, sine = fourier_parts(length, 1.0)
        return jnp.stack([jnp.stack([cosine, sine]), jnp.stack([-sine, cosine])])
    cosine, sine = fourier_parts(length, 1.0 / length)
    return jnp.stack([jnp.stack([cosine, -sine]), jnp.stack([sine, cosine])])


def along_rows(piece, table):
    return jnp.einsum("itzny,oikn->otzky", piece, table, precision=HIGHEST)


def along_depth(piece, table):
    return jnp.einsum("itnxy,oikn->otkxy", piece, table, precision=HIGHEST)


def on_device(record, shifts, station_group, weights, psf_real, psf_imag):
    per_station = station_counts(station_group)
    depth_rows = shifts.shape[1]
    lateral_rows = weights.shape[1]
    width_y = weights.shape[2]
    columns = lateral_rows * width_y
    first_time = lax.axis_index("sta") * T_DEV
    coefficient = coefficients(record, shifts, per_station, first_time, T_DEV)
    coefficient = coefficient.reshape(T_DEV * depth_rows, coefficient.shape[2])
    piece = lax.all_gather(weights, "sta", axis=0, tiled=True)
    stack = jnp.dot(
        coefficient, piece.reshape(piece.shape[0], columns), preferred_element_type=jnp.float32
    )
    stack = stack.reshape(T_DEV, depth_rows, lateral_rows, width_y)
    cosine_y, sine_y = fourier_parts(width_y, 1.0)
    spectrum = jnp.einsum(
        "tzxn,okn->otzxk", stack, jnp.stack([cosine_y, -sine_y]), precision=HIGHEST
    )
    row_table = complex_table(NX, True)
    by_rows = along_rows(
        lax.all_to_all(spectrum, "gy", split_axis=4, concat_axis=3, tiled=True), row_table
    )
    depth_table = complex_table(NZ, True)
    by_depth = along_depth(
        lax.all_to_all(by_rows, "gx", split_axis=3, concat_axis=2, tiled=True), depth_table
    )
    power = psf_real * psf_real + psf_imag * psf_imag + NOISE_POWER
    filt_real = (psf_real * by_depth[0] + psf_imag * by_depth[1]) / power
    filt_imag = (psf_real * by_depth[1] - psf_imag * by_depth[0]) / power
    back_depth = along_depth(jnp.stack([filt_real, filt_imag]), complex_table(NZ, False))
    back_table = complex_table(NX, False)
    back_rows = along_rows(
        lax.all_to_all(back_depth, "gx", split_axis=2, concat_axis=3, tiled=True), back_table
    )
    cosine_back, sine_back = fourier_parts(width_y, 1.0 / width_y)
    real_table = jnp.stack([cosine_back, -sine_back])
    return jnp.einsum(
        "itzxk,iyk->tzxy",
        lax.all_to_all(back_rows, "gy", split_axis=3, concat_axis=4, tiled=True),
        real_table,
        precision=HIGHEST,
    )


def solution(mesh):
    in_specs = (
        P(),
        P(None, "gx"),
        P(),
        P("sta", "gy", None),
        P(None, "gx", "gy"),
        P(None, "gx", "gy"),
    )
    out_specs = P("sta", "gx", "gy", None)
    return jax.shard_map(
        on_device, mesh=mesh, in_specs=in_specs, out_specs=out_specs, check_vma=False
    )
```

profile of v0, /device:TPU:0, one launch (start us, length us, event | category | flops | bytes accessed | tf_op | source)
XLA Modules:
  0.0 516.7 jit_solution(10342550417236700609)
XLA Ops:
  6.5 0.7 all-gather.2.cloned.1.call-update
  7.3 0.0 copy-done.4
  7.3 0.1 copy.50
  7.4 0.1 reshape.275
  7.5 0.1 copy-done
  7.6 16.6 %gather_fusion = f32[2048]{0:T(1024)S(1)} fusion(f32[128,1024]{1,0:T(8,128)S(1)} %copy-done, s32[2048]{0:T(1024)S(1)} %reshape.275), kind=kCustom, calls=%fused_computation | custom fusion | bytes 32768 | tf_op jit(solution)/shard_map/jit(take_along_axis)/gather | solution.py:25
  24.2 0.1 reshape.278
  24.3 0.1 convert_reduce_fusion
  24.5 0.1 convolution_bitcast_fusion.4
  24.6 4.1 fusion.27
  28.7 89.3 %all-gather.2.cloned.1.call-done = bf16[128,64,512]{2,1,0:T(8,128)(2,1)} async-done(((bf16[64,64,512]{2,1,0:T(8,128)(2,1)}), bf16[128,64,512]{2,1,0:T(8,128)(2,1)}) %all-gather.2.cloned.1.call-update) | async-done | bytes 8388624 | tf_op jit(solution)/shard_map/all_gather | solution.py:62
  118.0 13.1 %copy.78 = bf16[128,64,512]{0,2,1:T(8,128)(2,1)} copy(bf16[128,64,512]{2,1,0:T(8,128)(2,1)} %all-gather.2.cloned.1.call-done) | data formatting | bytes 16777216 | tf_op jit(solution)/shard_map/reshape | solution.py:64
  131.1 5.8 %fusion = f32[16,64,512]{2,0,1:T(8,128)S(1)} fusion(bf16[128,64,512]{0,2,1:T(8,128)(2,1)} %copy.78, f32[128,16]{1,0:T(8,128)S(1)} %reshape.278, s32[128,16]{1,0:T(8,128)S(1)} %copy.50, f32[128]{0:T(128)S(1)} %convolution_bitcast_fusion.4, s32[]{:T(128)S(6)} %axis_index.15), kind=kOutput, calls=%fused_computation.1 | convolution fusion | flops 134238208 | bytes 10502660 | tf_op jit(solution)/shard_map/dot_general | solution.py:63
  136.9 9.2 %convolution_bitcast_fusion = f32[2,1,16,64,512]{4,3,2,0,1:T(8,128)} fusion(f32[1,512,512]{2,1,0:T(8,128)S(1)} %get-tuple-element.12, f32[1,512,512]{2,1,0:T(8,128)S(1)} %get-tuple-element.11, f32[16,64,512]{2,0,1:T(8,128)S(1)} %fusion), kind=kOutput, calls=%fused_computation.8 | convolution fusion | flops 6442975232 | bytes 8388608 | tf_op jit(solution)/shard_map/tzxn,okn->otzxk/dot_general | solution.py:68
  146.0 9.1 %copy.54 = f32[2,1,16,64,512]{3,2,0,1,4:T(8,128)} copy(f32[2,1,16,64,512]{4,3,2,0,1:T(8,128)} %convolution_bitcast_fusion) | data formatting | bytes 8388608 | tf_op jit(solution)/shard_map/tzxn,okn->otzxk/transpose | solution.py:68
  155.2 19.9 %reshape.303 = f32[4,1,262144]{2,1,0:T(1,128)} reshape(f32[512,1,2,16,64]{4,3,2,1,0:T(8,128)} %bitcast.153) | data formatting | bytes 8388608
  175.1 4.8 all-to-all-start
  180.0 1.0 fusion.37
  180.9 1.0 fusion.35
  182.0 0.1 maximum_bitcast_fusion.15
  182.1 47.0 %all-to-all-done = f32[4,1,262144]{2,1,0:T(1,128)} async-done(((f32[4,1,262144]{2,1,0:T(1,128)}), f32[4,1,262144]{2,1,0:T(1,128)}, u32[]{:S(2)}, u32[]{:S(2)}) %all-to-all-start) | async-done | bytes 4194336 | tf_op jit(solution)/shard_map/all_to_all | solution.py:73
  229.1 0.5 broadcast.479
  229.6 15.2 %reduce = f32[4,262144]{1,0:T(4,128)} reduce(f32[4,1,262144]{2,1,0:T(1,128)} %all-to-all-done, f32[]{:T(128)} %broadcast.479), dimensions={1}, to_apply=%all_to_all.44.reduce_sub_computation | reduce | bytes 8388612 | tf_op jit(solution)/shard_map/all_to_all | solution.py:73
  244.8 9.3 %reshape.304 = f32[512,1,2,16,64]{4,3,2,1,0:T(8,128)} reshape(f32[4,262144]{1,0:T(4,128)} %reduce) | data formatting | bytes 8388608
  254.1 6.9 %copy.55 = f32[2,1,16,64,4,128]{5,3,4,0,2,1:T(8,128)} copy(f32[2,1,16,64,4,128]{3,2,0,5,4,1:T(8,128)} %bitcast.154) | data formatting | bytes 8388608 | tf_op jit(solution)/shard_map/all_to_all | solution.py:73
  261.0 8.7 %convolution_bitcast_fusion.3 = f32[2,1,16,256,128]{4,3,2,0,1:T(8,128)S(1)} fusion(f32[2,16,256,128,1]{3,2,0,1,4:T(8,128)} %bitcast.155, f32[1,2,256,256]{3,2,1,0:T(8,128)S(1)} %get-tuple-element.10, f32[1,2,256,256]{3,2,1,0:T(8,128)S(1)} %get-tuple-element.9), kind=kOutput, calls=%fused_computation.12 | convolution fusion | flops 6442713088 | bytes 9437184 | tf_op jit(solution)/shard_map/itzny,oikn->otzky/dot_general | solution.py:46
  269.7 4.4 copy.56
  274.1 6.9 %all-to-all-start.1 = ((f32[2,1,16,256,128]{4,2,0,1,3:T(8,128)}), f32[2,1,16,256,128]{4,2,0,1,3:T(8,128)}, u32[]{:S(2)}, u32[]{:S(2)}) async-start(f32[2,1,16,256,128]{4,2,0,1,3:T(8,128)} %copy.56), calls=%async_computation.1 | async-start | bytes 8388608 | tf_op jit(solution)/shard_map/all_to_all | solution.py:77
  281.0 1.0 fusion.38
  282.0 1.1 broadcast_multiply_fusion.1
  283.0 0.1 maximum_bitcast_fusion.13
  283.1 53.2 %all-to-all-done.1 = f32[2,1,16,256,128]{4,2,0,1,3:T(8,128)} async-done(((f32[2,1,16,256,128]{4,2,0,1,3:T(8,128)}), f32[2,1,16,256,128]{4,2,0,1,3:T(8,128)}, u32[]{:S(2)}, u32[]{:S(2)}) %all-to-all-start.1) | async-done | bytes 4194336 | tf_op jit(solution)/shard_map/all_to_all | solution.py:77
  336.3 2.7 copy.57
  339.0 0.0 copy-start.2
  339.1 7.1 %convolution_bitcast_fusion.2 = f32[2,256,16,128]{3,1,2,0:T(8,128)S(1)} fusion(f32[2,256,16,128,1]{3,1,0,2,4:T(8,128)S(1)} %bitcast.157, f32[1,2,256,256]{3,2,1,0:T(8,128)S(1)} %get-tuple-element.10, f32[1,2,256,256]{3,2,1,0:T(8,128)S(1)} %get-tuple-element.9), kind=kOutput, calls=%fused_computation.11 | convolution fusion | flops 6442713088 | bytes 9437184 | tf_op jit(solution)/shard_map/itnxy,oikn->otkxy/dot_general | solution.py:50
  346.2 1.5 fusion.13
  347.7 7.3 %fusion.5 = f32[2,1,256,16,128]{4,2,3,0,1:T(8,128)S(1)} fusion(f32[1,2,256,256]{3,2,1,0:T(8,128)S(1)} %get-tuple-element.8, f32[1,2,256,256]{3,2,1,0:T(8,128)S(1)} %get-tuple-element.7, f32[1,1,256,16,128]{4,2,3,1,0:T(8,128)S(1)} %get-tuple-element.6, f32[1,1,256,16,128]{4,2,3,1,0:T(8,128)S(1)} %get-tuple-element.5), kind=kOutput, calls=%fused_computation.9 | convolution fusion | flops 6443761664 | bytes 9437184 | tf_op jit(solution)/shard_map/itnxy,oikn->otkxy/dot_general | solution.py:50
  355.0 2.4 copy.64
  357.5 64.3 %all_to_all.60 = f32[2,1,256,16,128]{4,3,0,1,2:T(8,128)S(1)} all-to-all(f32[2,1,256,16,128]{4,3,0,1,2:T(8,128)S(1)} %copy.64), channel_id=1, replica_groups=mesh['sta'=2,'gx'=16,'gy'=4] {'gx'}, dimensions={2} | all-to-all | bytes 8388608 | tf_op jit(solution)/shard_map/all_to_all | solution.py:85
  421.8 0.5 copy.65
  422.3 6.9 %convolution_bitcast_fusion.1 = f32[2,1,16,256,128]{4,3,2,0,1:T(8,128)S(1)} fusion(f32[2,16,256,128,1]{3,2,0,1,4:T(8,128)S(1)} %bitcast.156, f32[1,2,256,256]{3,2,1,0:T(8,128)S(1)} %get-tuple-element.8, f32[1,2,256,256]{3,2,1,0:T(8,128)S(1)} %get-tuple-element.7), kind=kOutput, calls=%fused_computation.10 | convolution fusion | flops 6442713088 | bytes 9437184 | tf_op jit(solution)/shard_map/itzny,oikn->otzky/dot_general | solution.py:46
  429.2 4.4 copy.66
  433.6 5.1 all-to-all-start.3
  438.7 4.2 multiply_negate_fusion
  442.8 44.5 %all-to-all-done.3 = f32[2,1,16,256,128]{4,2,0,1,3:T(8,128)} async-done(((f32[2,1,16,256,128]{4,2,0,1,3:T(8,128)}), f32[2,1,16,256,128]{4,2,0,1,3:T(8,128)}, u32[]{:S(2)}, u32[]{:S(2)}) %all-to-all-start.3) | async-done | bytes 4194336 | tf_op jit(solution)/shard_map/all_to_all | solution.py:91
  487.3 6.9 %copy.94 = f32[2,1,16,4,64,128]{5,3,4,0,2,1:T(4,128)} copy(f32[2,1,16,4,64,128]{5,2,0,4,3,1:T(8,128)} %bitcast.57) | data formatting | bytes 8388608 | tf_op jit(solution)/shard_map/all_to_all | solution.py:91
  494.2 5.5 %reshape.274 = f32[2,16,64,512]{3,2,0,1:T(8,128)} reshape(f32[2,1,16,64,4,128]{5,4,3,0,2,1:T(4,128)} %bitcast.159) | data formatting | bytes 8388608 | tf_op jit(solution)/shard_map/reshape.27
  499.7 9.9 %fusion.19 = f32[1,16,64,512]{3,2,1,0:T(8,128)} fusion(f32[2,16,64,512]{3,2,0,1:T(8,128)} %reshape.274, f32[1,512,512]{2,1,0:T(8,128)S(1)} %get-tuple-element.17, f32[1,512,512]{2,1,0:T(8,128)S(1)} %get-tuple-element.18), kind=kOutput, calls=%fused_computation.33 | convolution fusion | flops 6442975232 | bytes 8388608 | tf_op jit(solution)/shard_map/itzxk,iyk->tzxy/dot_general | solution.py:89
  (11 shorter events, 0.0 us)
Async XLA Ops:
  6.5 1.1 copy-start
  6.5 0.8 copy-start.4
  6.5 111.5 %all-gather.2.cloned.1.call-start = ((), (), s32[]{:S(2)}) async-start(), calls=%async_computation.4 | async-start | bytes 12582912 | tf_op jit(solution)/shard_map/all_gather | solution.py:62
  7.6 16.7 %copy-start.5 = (s32[128]{0:T(128)S(1)}, s32[128]{0:T(128)}, u32[]{:S(2)}) copy-start(s32[128]{0:T(128)} %param.8) | copy-start | bytes 1540
  175.1 54.0 %all-to-all-start = ((f32[4,1,262144]{2,1,0:T(1,128)}), f32[4,1,262144]{2,1,0:T(1,128)}, u32[]{:S(2)}, u32[]{:S(2)}) async-start(f32[4,1,262144]{2,1,0:T(1,128)} %reshape.303), calls=%async_computation | async-start | bytes 8388608 | tf_op jit(solution)/shard_map/all_to_all | solution.py:73
  274.1 62.2 %all-to-all-start.1 = ((f32[2,1,16,256,128]{4,2,0,1,3:T(8,128)}), f32[2,1,16,256,128]{4,2,0,1,3:T(8,128)}, u32[]{:S(2)}, u32[]{:S(2)}) async-start(f32[2,1,16,256,128]{4,2,0,1,3:T(8,128)} %copy.56), calls=%async_computation.1 | async-start | bytes 8388608 | tf_op jit(solution)/shard_map/all_to_all | solution.py:77
  339.0 7.2 %copy-start.2 = (f32[256,16,128]{2,1,0:T(8,128)S(1)}, f32[256,16,128]{2,1,0:T(8,128)}, u32[]{:S(2)}) copy-start(f32[256,16,128]{2,1,0:T(8,128)} %param.11) | copy-start | bytes 6291460
  339.0 7.2 %copy-start.3 = (f32[256,16,128]{2,1,0:T(8,128)S(1)}, f32[256,16,128]{2,1,0:T(8,128)}, u32[]{:S(2)}) copy-start(f32[256,16,128]{2,1,0:T(8,128)} %param.10) | copy-start | bytes 6291460
  433.6 53.7 %all-to-all-start.3 = ((f32[2,1,16,256,128]{4,2,0,1,3:T(8,128)}), f32[2,1,16,256,128]{4,2,0,1,3:T(8,128)}, u32[]{:S(2)}, u32[]{:S(2)}) async-start(f32[2,1,16,256,128]{4,2,0,1,3:T(8,128)} %copy.66), calls=%async_computation.3 | async-start | bytes 8388608 | tf_op jit(solution)/shard_map/all_to_all | solution.py:91
  499.7 9.9 %copy-start.1 = (f32[128,1024]{1,0:T(8,128)S(1)}, f32[128,1024]{1,0:T(8,128)}, u32[]{:S(2)}) copy-start(f32[128,1024]{1,0:T(8,128)} %param.6) | copy-start | bytes 1572868
Sparse Core Ops, SparseCore 0:
  9.0 108.9 all-gather.1
where the time goes:
time: 526 us; the launch traced here: 517 us
  waiting for transfers between devices  235 us (45%)
  local copies, waits for them, and re-layouts  103 us (20%)
  blocking collectives  64.3 us (12%)
  matrix products  55 us (10%)
  other arithmetic  29.4 us (6%)
  starting transfers between devices  16.8 us (3%)
  between operations  13.8 us (3%)
    all_gather x1, waiting for transfers between devices, on_device(): piece = lax.all_gather(weights, 'sta', axis=0, tiled=True)  89.3 us
    all_to_all x1, blocking collectives, on_device(): lax.all_to_all(back_depth, 'gx', split_axis=2, concat_axis=3, tiled=True)  64.3 us
    all_to_all x1, waiting for transfers between devices, on_device(): lax.all_to_all(by_rows, 'gx', split_axis=3, concat_axis=2, tiled=True)  53.2 us
    all_to_all x1, waiting for transfers between devices, on_device(): lax.all_to_all(spectrum, 'gy', split_axis=4, concat_axis=3, tiled=True)  47 us
    all_to_all x1, waiting for transfers between devices, on_device(): lax.all_to_all(back_rows, 'gy', split_axis=3, concat_axis=4, tiled=True)  44.5 us
    unnamed x15, local copies, waits for them, and re-layouts  29.4 us
    gather x3, local copies, waits for them, and re-layouts, coefficients(): jnp.take_along_axis(record, positions.reshape(positions.shape[0], -1), ax...  16.8 us
    dot_general x2, matrix products, along_rows(): return jnp.einsum('itzny,oikn->otzky', piece, table, precision=HIGHEST)  15.6 us
  transfers between devices with their start and end apart: 4, of which 4 were waited for; matrix products, arithmetic and copies ran while one was open for 6% of the time, Pallas kernels for 0%

commit v1 on v0

--- a/solution.py
+++ b/solution.py
@@ -10,6 +10,35 @@
 GROUPS = 8
 NOISE_POWER = 0.25
 HIGHEST = lax.Precision.HIGHEST
+
+
+def draft_stacks_all(v0, out_dim, xx):
+    inter = v0.shape
+    t_next = v0.reshape(*inter[:out_dim], xx, inter[out_dim] // xx, *inter[out_dim + 1 :])
+    return jnp.moveaxis(t_next, out_dim, 0)
+
+
+def finish_terms(row_data, dimension_no):
+    row_data = jnp.moveaxis(row_data, 0, dimension_no)
+    y2 = row_data.shape
+    return row_data.reshape(
+        *y2[:dimension_no], y2[dimension_no] * y2[dimension_no + 1], *y2[dimension_no + 2 :]
+    )
+
+
+def scan_surface_for(state, lane_axis, patch, w_in):
+    outer = lax.axis_size(lane_axis)
+    z = lax.axis_index(lane_axis)
+    mid_arr, fresh = (outer, z)
+    outcome_arr = draft_stacks_all(state, patch, mid_arr)
+    history = [outcome_arr[fresh]]
+    for dev_j in range(1, mid_arr):
+        item_now = outcome_arr[fresh ^ dev_j]
+        b_next = lax.ppermute(item_now, lane_axis, [(num, num ^ dev_j) for num in range(mid_arr)])
+        history.append(b_next)
+    right_arr = jnp.stack(history, axis=0)
+    outcome_arr = right_arr[fresh ^ jnp.arange(mid_arr)]
+    return finish_terms(outcome_arr, w_in)
 
 
 def station_counts(station_group):
@@ -69,9 +98,7 @@
         "tzxn,okn->otzxk", stack, jnp.stack([cosine_y, -sine_y]), precision=HIGHEST
     )
     row_table = complex_table(NX, True)
-    by_rows = along_rows(
-        lax.all_to_all(spectrum, "gy", split_axis=4, concat_axis=3, tiled=True), row_table
-    )
+    by_rows = along_rows(scan_surface_for(spectrum, "gy", 4, 3), row_table)
     depth_table = complex_table(NZ, True)
     by_depth = along_depth(
         lax.all_to_all(by_rows, "gx", split_axis=3, concat_axis=2, tiled=True), depth_table

time: 526 us -> 496 us (0.943)
  other arithmetic: 29.4 us -> 16.4 us
  local copies, waits for them, and re-layouts: 103 us -> 92.8 us
    all_to_all x1 -> x0, waiting for transfers between devices: 47 us -> none  [on_device(): lax.all_to_all(spectrum, 'gy', split_axis=4, concat_axis=3, tiled=True)]
    ppermute x0 -> x3, waiting for transfers between devices: none -> 43 us  [scan_surface_for(): lax.ppermute(item_now, lane_axis, [(num, num ^ dev_j) for num in range(mi...]
    unnamed x15 -> x13, local copies, waits for them, and re-layouts: 29.4 us -> 0.22 us
    reshape x0 -> x1, local copies, waits for them, and re-layouts: none -> 17.2 us  [draft_stacks_all(): v0.reshape(*inter[:out_dim], xx, inter[out_dim] // xx, *inter[out_dim + 1:])]
    all_to_all x1 -> x0, other arithmetic: 15.2 us -> none  [on_device(): lax.all_to_all(spectrum, 'gy', split_axis=4, concat_axis=3, tiled=True)]
    another operation x1 -> x2, local copies, waits for them, and re-layouts: 5.49 us -> 16.2 us
    all_to_all x2 -> x0, local copies, waits for them, and re-layouts: 7.36 us -> none  [on_device(): lax.all_to_all(spectrum, 'gy', split_axis=4, concat_axis=3, tiled=True)]
    transpose x1, local copies, waits for them, and re-layouts: 9.13 us -> 2.49 us  [finish_terms(): row_data = jnp.moveaxis(row_data, 0, dimension_no)]
  transfers between devices with their start and end apart: 4 -> 6, of which waited for: 4 -> 5; matrix products, arithmetic and copies ran while one was open for 6% -> 6% of each run, Pallas kernels for 0% -> 0%
where the time goes in v1:
time: 496 us; the launch traced here: 487 us
  waiting for transfers between devices  231 us (47%)
  local copies, waits for them, and re-layouts  92.8 us (19%)
  blocking collectives  64.4 us (13%)
  matrix products  52.9 us (11%)
  other arithmetic  16.4 us (3%)
  starting transfers between devices  16 us (3%)
  between operations  14.1 us (3%)
    all_gather x1, waiting for transfers between devices, on_device(): piece = lax.all_gather(weights, 'sta', axis=0, tiled=True)  89.3 us
    all_to_all x1, blocking collectives, on_device(): lax.all_to_all(back_depth, 'gx', split_axis=2, concat_axis=3, tiled=True)  64.4 us
    all_to_all x1, waiting for transfers between devices, on_device(): lax.all_to_all(by_rows, 'gx', split_axis=3, concat_axis=2, tiled=True)  53.4 us
    all_to_all x1, waiting for transfers between devices, on_device(): lax.all_to_all(back_rows, 'gy', split_axis=3, concat_axis=4, tiled=True)  44.5 us
    ppermute x3, waiting for transfers between devices, scan_surface_for(): lax.ppermute(item_now, lane_axis, [(num, num ^ dev_j) for num in range(mi...  43 us
    reshape x1, local copies, waits for them, and re-layouts, draft_stacks_all(): v0.reshape(*inter[:out_dim], xx, inter[out_dim] // xx, *inter[out_dim + 1:])  17.2 us
    gather x3, local copies, waits for them, and re-layouts, coefficients(): jnp.take_along_axis(record, positions.reshape(positions.shape[0], -1), ax...  16.8 us
    another operation x2, local copies, waits for them, and re-layouts  16.2 us
  transfers between devices with their start and end apart: 6, of which 5 were waited for; matrix products, arithmetic and copies ran while one was open for 6% of the time, Pallas kernels for 0%

profile of v1, /device:TPU:0, one launch (start us, length us, event | category | flops | bytes accessed | tf_op | source)
XLA Modules:
  0.0 487.3 jit_solution(2113954405603891690)
XLA Ops:
  6.5 0.7 all-gather.2.cloned.1.call-update
  7.3 0.1 copy.64
  7.4 0.1 reshape.313
  7.5 0.1 copy-done
  7.6 16.6 %gather_fusion.1 = f32[2048]{0:T(1024)S(1)} fusion(f32[128,1024]{1,0:T(8,128)S(1)} %copy-done, s32[2048]{0:T(1024)S(1)} %reshape.313), kind=kCustom, calls=%fused_computation.1 | custom fusion | bytes 32768 | tf_op jit(solution)/shard_map/jit(take_along_axis)/gather | solution.py:54
  24.2 0.1 reshape.316
  24.4 0.1 convert_reduce_fusion
  24.5 0.1 convolution_bitcast_fusion.3
  24.6 4.1 fusion.33
  28.7 89.3 %all-gather.2.cloned.1.call-done = bf16[128,64,512]{2,1,0:T(8,128)(2,1)} async-done(((bf16[64,64,512]{2,1,0:T(8,128)(2,1)}), bf16[128,64,512]{2,1,0:T(8,128)(2,1)}) %all-gather.2.cloned.1.call-update) | async-done | bytes 8388624 | tf_op jit(solution)/shard_map/all_gather | solution.py:91
  118.0 13.0 %copy.92 = bf16[128,64,512]{0,2,1:T(8,128)(2,1)} copy(bf16[128,64,512]{2,1,0:T(8,128)(2,1)} %all-gather.2.cloned.1.call-done) | data formatting | bytes 16777216 | tf_op jit(solution)/shard_map/reshape | solution.py:93
  131.0 5.8 %fusion = f32[16,64,512]{2,0,1:T(8,128)S(1)} fusion(bf16[128,64,512]{0,2,1:T(8,128)(2,1)} %copy.92, f32[128,16]{1,0:T(8,128)S(1)} %reshape.316, s32[128,16]{1,0:T(8,128)S(1)} %copy.64, f32[128]{0:T(128)S(1)} %convolution_bitcast_fusion.3, s32[]{:T(128)S(6)} %axis_index.23), kind=kOutput, calls=%fused_computation.2 | convolution fusion | flops 134238208 | bytes 10502660 | tf_op jit(solution)/shard_map/dot_general | solution.py:92
  136.8 9.2 %convolution_bitcast_fusion = f32[2,1,16,64,512]{4,3,2,0,1:T(8,128)} fusion(f32[1,512,512]{2,1,0:T(8,128)S(1)} %get-tuple-element.16, f32[1,512,512]{2,1,0:T(8,128)S(1)} %get-tuple-element.15, f32[16,64,512]{2,0,1:T(8,128)S(1)} %fusion), kind=kOutput, calls=%fused_computation.13 | convolution fusion | flops 6442975232 | bytes 8388608 | tf_op jit(solution)/shard_map/tzxn,okn->otzxk/dot_general | solution.py:97
  145.9 17.2 %reshape.297 = f32[2,1,16,64,4,128]{5,4,3,2,0,1:T(4,128)} reshape(f32[2,1,16,64,512]{4,3,2,0,1:T(8,128)} %convolution_bitcast_fusion) | data formatting | bytes 8388608 | tf_op jit(solution)/shard_map/reshape | solution.py:17
  163.1 10.8 %constant_dynamic-slice_fusion.3 = (f32[2,1,16,64,1,128]{5,4,3,2,0,1:T(1,128)S(1)}, f32[2,1,16,64,1,128]{5,4,3,2,0,1:T(1,128)S(1)}, f32[2,1,16,64,1,128]{5,4,3,2,0,1:T(1,128)S(1)}, f32[2,1,16,64,1,128]{5,4,3,2,0,1:T(1,128)S(1)}) fusion(f32[2,1,16,64,4,128]{5,4,3,2,0,1:T(4,128)} %reshape.297, s32[]{:T(128)S(6)} %select_n.128, s32[]{:T(128)S(6)} %select_n.131, ...), kind=kLoop, calls=%fused_computation.92 | loop fusion | bytes 8388624 | tf_op jit(solution)/shard_map/dynamic-slice
  173.9 2.8 collective-permute-start.2
  176.7 0.8 collective-permute-start.1
  177.6 0.5 collective-permute-start
  178.1 1.0 fusion.43
  179.1 1.0 fusion.41
  180.1 0.1 maximum_bitcast_fusion.16
  180.2 42.4 %collective-permute-done.2 = f32[2,1,16,64,128]{4,3,2,0,1:T(8,128)S(1)} collective-permute-done((f32[2,1,16,64,128]{4,3,2,0,1:T(8,128)S(1)}, f32[2,1,16,64,128]{4,3,2,0,1:T(8,128)S(1)}, u32[]{:S(2)}, u32[]{:S(2)}) %collective-permute-start.2) | collective-permute-done | bytes 1048608 | tf_op jit(solution)/shard_map/ppermute | solution.py:37
  222.6 0.6 collective-permute-done
  223.2 2.3 maximum_bitcast_fusion
  225.5 5.0 %gather_fusion = f32[4,2,16,64,128]{4,3,2,1,0:T(8,128)} fusion(f32[4,2,16,64,128]{4,3,2,1,0:T(8,128)} %maximum_bitcast_fusion, s32[1024]{0:T(1024)S(1)} %pad_clamp_fusion), kind=kCustom, calls=%fused_computation | custom fusion | bytes 8388624 | tf_op jit(solution)/shard_map/gather | solution.py:40
  230.5 2.5 copy.68
  232.9 6.8 %fusion.8 = f32[2,1,16,256,128]{4,3,2,0,1:T(8,128)S(1)} fusion(f32[2,16,256,128]{3,2,1,0:T(8,128)S(1)} %bitcast.169, f32[1,2,256,256]{3,2,1,0:T(8,128)S(1)} %get-tuple-element.14, f32[1,2,256,256]{3,2,1,0:T(8,128)S(1)} %get-tuple-element.13), kind=kOutput, calls=%fused_computation.14 | convolution fusion | flops 6442713088 | bytes 9437184 | tf_op jit(solution)/shard_map/itzny,oikn->otzky/dot_general | solution.py:75
  239.8 4.8 copy.70
  244.6 6.7 %all-to-all-start = ((f32[2,1,16,256,128]{4,2,0,1,3:T(8,128)}), f32[2,1,16,256,128]{4,2,0,1,3:T(8,128)}, u32[]{:S(2)}, u32[]{:S(2)}) async-start(f32[2,1,16,256,128]{4,2,0,1,3:T(8,128)} %copy.70), calls=%async_computation | async-start | bytes 8388608 | tf_op jit(solution)/shard_map/all_to_all | solution.py:104
  251.3 1.0 fusion.44
  252.3 1.1 broadcast_multiply_fusion.1
  253.4 0.1 maximum_bitcast_fusion.14
  253.5 53.4 %all-to-all-done = f32[2,1,16,256,128]{4,2,0,1,3:T(8,128)} async-done(((f32[2,1,16,256,128]{4,2,0,1,3:T(8,128)}), f32[2,1,16,256,128]{4,2,0,1,3:T(8,128)}, u32[]{:S(2)}, u32[]{:S(2)}) %all-to-all-start) | async-done | bytes 4194336 | tf_op jit(solution)/shard_map/all_to_all | solution.py:104
  306.8 2.7 copy.71
  309.6 7.1 %convolution_bitcast_fusion.2 = f32[2,256,16,128]{3,1,2,0:T(8,128)S(1)} fusion(f32[2,256,16,128,1]{3,1,0,2,4:T(8,128)S(1)} %bitcast.170, f32[1,2,256,256]{3,2,1,0:T(8,128)S(1)} %get-tuple-element.14, f32[1,2,256,256]{3,2,1,0:T(8,128)S(1)} %get-tuple-element.13), kind=kOutput, calls=%fused_computation.17 | convolution fusion | flops 6442713088 | bytes 9437184 | tf_op jit(solution)/shard_map/itnxy,oikn->otkxy/dot_general | solution.py:79
  316.8 1.5 fusion.19
  318.3 7.1 %fusion.11 = f32[2,1,256,16,128]{4,2,3,0,1:T(8,128)S(1)} fusion(f32[1,2,256,256]{3,2,1,0:T(8,128)S(1)} %get-tuple-element.12, f32[1,2,256,256]{3,2,1,0:T(8,128)S(1)} %get-tuple-element.11, f32[1,1,256,16,128]{4,2,3,1,0:T(8,128)S(1)} %get-tuple-element.6, f32[1,1,256,16,128]{4,2,3,1,0:T(8,128)S(1)} %get-tuple-element.5), kind=kOutput, calls=%fused_computation.15 | convolution fusion | flops 6443761664 | bytes 9437184 | tf_op jit(solution)/shard_map/itnxy,oikn->otkxy/dot_general | solution.py:79
  325.3 2.4 copy.78
  327.8 64.4 %all_to_all.45 = f32[2,1,256,16,128]{4,3,0,1,2:T(8,128)S(1)} all-to-all(f32[2,1,256,16,128]{4,3,0,1,2:T(8,128)S(1)} %copy.78), channel_id=1, replica_groups=mesh['sta'=2,'gx'=16,'gy'=4] {'gx'}, dimensions={2} | all-to-all | bytes 8388608 | tf_op jit(solution)/shard_map/all_to_all | solution.py:112
  392.1 0.5 copy.79
  392.7 6.9 %convolution_bitcast_fusion.1 = f32[2,1,16,256,128]{4,3,2,0,1:T(8,128)S(1)} fusion(f32[2,16,256,128,1]{3,2,0,1,4:T(8,128)S(1)} %bitcast.168, f32[1,2,256,256]{3,2,1,0:T(8,128)S(1)} %get-tuple-element.12, f32[1,2,256,256]{3,2,1,0:T(8,128)S(1)} %get-tuple-element.11), kind=kOutput, calls=%fused_computation.16 | convolution fusion | flops 6442713088 | bytes 9437184 | tf_op jit(solution)/shard_map/itzny,oikn->otzky/dot_general | solution.py:75
  399.5 4.4 copy.80
  404.0 5.1 %all-to-all-start.2 = ((f32[2,1,16,256,128]{4,2,0,1,3:T(8,128)}), f32[2,1,16,256,128]{4,2,0,1,3:T(8,128)}, u32[]{:S(2)}, u32[]{:S(2)}) async-start(f32[2,1,16,256,128]{4,2,0,1,3:T(8,128)} %copy.80), calls=%async_computation.2 | async-start | bytes 8388608 | tf_op jit(solution)/shard_map/all_to_all | solution.py:118
  409.1 4.2 multiply_negate_fusion
  413.2 44.5 %all-to-all-done.2 = f32[2,1,16,256,128]{4,2,0,1,3:T(8,128)} async-done(((f32[2,1,16,256,128]{4,2,0,1,3:T(8,128)}), f32[2,1,16,256,128]{4,2,0,1,3:T(8,128)}, u32[]{:S(2)}, u32[]{:S(2)}) %all-to-all-start.2) | async-done | bytes 4194336 | tf_op jit(solution)/shard_map/all_to_all | solution.py:118
  457.7 6.9 %copy.114 = f32[2,1,16,4,64,128]{5,3,4,0,2,1:T(4,128)} copy(f32[2,1,16,4,64,128]{5,2,0,4,3,1:T(8,128)} %bitcast.66) | data formatting | bytes 8388608 | tf_op jit(solution)/shard_map/all_to_all | solution.py:118
  464.6 5.5 %reshape.302 = f32[2,16,64,512]{3,2,0,1:T(8,128)} reshape(f32[2,1,16,64,4,128]{5,4,3,0,2,1:T(4,128)} %bitcast.173) | data formatting | bytes 8388608 | tf_op jit(solution)/shard_map/reshape.29
  470.1 9.9 %fusion.25 = f32[1,16,64,512]{3,2,1,0:T(8,128)} fusion(f32[2,16,64,512]{3,2,0,1:T(8,128)} %reshape.302, f32[1,512,512]{2,1,0:T(8,128)S(1)} %get-tuple-element.21, f32[1,512,512]{2,1,0:T(8,128)S(1)} %get-tuple-element.22), kind=kOutput, calls=%fused_computation.38 | convolution fusion | flops 6442975232 | bytes 8388608 | tf_op jit(solution)/shard_map/itzxk,iyk->tzxy/dot_general | solution.py:116
  (16 shorter events, 0.1 us)
Async XLA Ops:
  6.5 1.1 copy-start
  6.5 0.8 copy-start.4
  6.5 111.5 %all-gather.2.cloned.1.call-start = ((), (), s32[]{:S(2)}) async-start(), calls=%async_computation.3 | async-start | bytes 12582912 | tf_op jit(solution)/shard_map/all_gather | solution.py:91
  7.6 16.8 %copy-start.5 = (s32[128]{0:T(128)S(1)}, s32[128]{0:T(128)}, u32[]{:S(2)}) copy-start(s32[128]{0:T(128)} %param.8) | copy-start | bytes 1540
  173.9 48.7 %collective-permute-start.2 = (f32[2,1,16,64,128]{4,3,2,0,1:T(8,128)S(1)}, f32[2,1,16,64,128]{4,3,2,0,1:T(8,128)S(1)}, u32[]{:S(2)}, u32[]{:S(2)}) collective-permute-start(f32[2,1,16,64,128]{4,3,2,0,1:T(8,128)S(1)} %bitcast.177), channel_id=1, source_target_pairs={{0,3},{1,2},{2,1},{3,0},{4,7},{5,6},{6,5},{7,4},{8,11},{9,10},{10,... | collective-permute-start | bytes 3145736 | tf_op jit(solution)/shard_map/ppermute | solution.py:37
  176.7 45.8 %collective-permute-start.1 = (f32[2,1,16,64,128]{4,3,2,0,1:T(8,128)S(1)}, f32[2,1,16,64,128]{4,3,2,0,1:T(8,128)S(1)}, u32[]{:S(2)}, u32[]{:S(2)}) collective-permute-start(f32[2,1,16,64,128]{4,3,2,0,1:T(8,128)S(1)} %bitcast.176), channel_id=1, source_target_pairs={{0,2},{1,3},{2,0},{3,1},{4,6},{5,7},{6,4},{7,5},{8,10},{9,11},{10,... | collective-permute-start | bytes 3145736 | tf_op jit(solution)/shard_map/ppermute | solution.py:37
  177.6 45.6 %collective-permute-start = (f32[2,1,16,64,128]{4,3,2,0,1:T(8,128)S(1)}, f32[2,1,16,64,128]{4,3,2,0,1:T(8,128)S(1)}, u32[]{:S(2)}, u32[]{:S(2)}) collective-permute-start(f32[2,1,16,64,128]{4,3,2,0,1:T(8,128)S(1)} %bitcast.175), channel_id=1, source_target_pairs={{0,1},{1,0},{2,3},{3,2},{4,5},{5,4},{6,7},{7,6},{8,9},{9,8},{10,11... | collective-permute-start | bytes 3145736 | tf_op jit(solution)/shard_map/ppermute | solution.py:37
  244.6 62.2 %all-to-all-start = ((f32[2,1,16,256,128]{4,2,0,1,3:T(8,128)}), f32[2,1,16,256,128]{4,2,0,1,3:T(8,128)}, u32[]{:S(2)}, u32[]{:S(2)}) async-start(f32[2,1,16,256,128]{4,2,0,1,3:T(8,128)} %copy.70), calls=%async_computation | async-start | bytes 8388608 | tf_op jit(solution)/shard_map/all_to_all | solution.py:104
  309.6 7.2 %copy-start.2 = (f32[256,16,128]{2,1,0:T(8,128)S(1)}, f32[256,16,128]{2,1,0:T(8,128)}, u32[]{:S(2)}) copy-start(f32[256,16,128]{2,1,0:T(8,128)} %param.11) | copy-start | bytes 6291460
  309.6 7.2 %copy-start.3 = (f32[256,16,128]{2,1,0:T(8,128)S(1)}, f32[256,16,128]{2,1,0:T(8,128)}, u32[]{:S(2)}) copy-start(f32[256,16,128]{2,1,0:T(8,128)} %param.10) | copy-start | bytes 6291460
  404.0 53.7 %all-to-all-start.2 = ((f32[2,1,16,256,128]{4,2,0,1,3:T(8,128)}), f32[2,1,16,256,128]{4,2,0,1,3:T(8,128)}, u32[]{:S(2)}, u32[]{:S(2)}) async-start(f32[2,1,16,256,128]{4,2,0,1,3:T(8,128)} %copy.80), calls=%async_computation.2 | async-start | bytes 8388608 | tf_op jit(solution)/shard_map/all_to_all | solution.py:118
  470.1 9.9 %copy-start.1 = (f32[128,1024]{1,0:T(8,128)S(1)}, f32[128,1024]{1,0:T(8,128)}, u32[]{:S(2)}) copy-start(f32[128,1024]{1,0:T(8,128)} %param.6) | copy-start | bytes 1572868
Sparse Core Ops, SparseCore 0:
  9.0 108.9 all-gather.1
